TPU v7x, 128 devices: a whole 4x4x4 slice. The times are simulated.
128 devices in a mesh: chan: 16 (over y_lo, z, core), band: 8 (over x, y_hi).
Axes of the slice: x: 4, y: 4 (y_hi: 2, y_lo: 2; y = y_hi * 2 + y_lo), z: 4, core: 2. Of those that a mesh axis runs over, the one named last changes fastest.
Arguments:
- raw: bfloat16 [128, 2560, 2747], P(('chan', 'band')), may hold values from -600 to 600
- offsets: int32 [128], P(('chan', 'band')), may hold values from 0 to 127
- taps: bfloat16 [63], replicated, may hold values from -0.75 to 0.75
- partner: int32 [2, 16], replicated, may hold values from 0 to 15, as said below
Outputs:
- cross: float32 [2, 2, 128, 2560, 160], P(None, None, 'band', 'chan')
Inputs may be any that keep to these rules, and one draw needn't show every extreme that they name: For each round r there is one number M of 1 to 15 with partner[r, a] = a xor M for every block a; the two rounds' numbers differ.
All inputs are finite; a program needn't handle non-finite values.
Results may differ from a plain program's by a relative error of at most 0.0041.
Values may be sent and summed in bfloat16 or wider, within the bound.
No kernel may reach another device: no remote copies, remote signals or barrier semaphores. Data moves between devices by JAX's collectives and lax.ppermute only.
A program may use at most 128 MiB of HBM per device.

v0:
```python
import math
import jax
import jax.numpy as jnp
from jax import lax
from jax.sharding import PartitionSpec as P

DEC = 10
TAPS = 63
W = 256
NF = 128
HALF = 32


def mean_matrix(length, half):
    rows = jnp.arange(length, dtype=jnp.int32)[:, None]
    cols = jnp.arange(length, dtype=jnp.int32)[None, :]
    begins = jnp.clip(cols - half, 0, length - 2 * half - 1)
    inside = (rows >= begins) & (rows <= begins + 2 * half)
    return inside.astype(jnp.float32)


def dft_table(length, bins):
    samples = jnp.arange(length, dtype=jnp.int32)[:, None]
    freqs = jnp.arange(bins, dtype=jnp.int32)[None, :]
    phase = samples * freqs % length
    angle = phase.astype(jnp.float32) * (2.0 * math.pi / length)
    return jnp.concatenate([jnp.cos(angle), -jnp.sin(angle)], axis=1)


def filter_table(taps, phases):
    padded = jnp.pad(taps, (0, phases * DEC - TAPS))
    grid = padded.reshape(phases, DEC)
    rows = jnp.arange(W + phases - 1, dtype=jnp.int32)[:, None]
    cols = jnp.arange(W, dtype=jnp.int32)[None, :]
    onehot = (
        (rows - cols)[None, :, :] == jnp.arange(phases, dtype=jnp.int32)[:, None, None]
    ).astype(jnp.bfloat16)
    table = jnp.einsum("jqn,jr->qrn", onehot, grid, preferred_element_type=jnp.float32)
    return table.reshape((W + phases - 1) * DEC, W).astype(jnp.bfloat16)


def window_spectrum(segment, offset, table, level_matrix, transform):
    span = table.shape[0]
    piece = lax.dynamic_slice_in_dim(segment, offset, span, 1)
    decimated = jnp.dot(piece, table, preferred_element_type=jnp.float32)
    level = jnp.dot(jnp.abs(decimated), level_matrix, precision=lax.Precision.HIGHEST) / (
        2 * HALF + 1
    )
    normed = decimated / (level + 1e-05)
    spectrum = lax.dot_general(
        transform, normed, (((0,), (1,)), ((), ())), precision=lax.Precision.HIGHEST
    )
    return spectrum.reshape(2, NF, segment.shape[0]).astype(jnp.bfloat16)


def body(raw, offsets, taps, partner):
    phases = (TAPS + DEC - 1) // DEC
    table = filter_table(taps, phases)
    level_matrix = mean_matrix(W, HALF)
    transform = dft_table(W, NF)
    spectra = jnp.stack([window_spectrum(raw[0], offsets[0], table, level_matrix, transform)])
    chan_count = lax.axis_size("chan")
    band_count = lax.axis_size("band")
    window_count, part_count, bin_count, channel_count = spectra.shape
    arranged = spectra.reshape(
        window_count,
        part_count,
        band_count,
        bin_count // band_count,
        chan_count,
        channel_count // chan_count,
    )
    arranged = arranged.transpose(4, 2, 0, 1, 3, 5).reshape(
        chan_count * band_count * window_count,
        part_count,
        bin_count // band_count,
        channel_count // chan_count,
    )
    local = lax.all_to_all(arranged, ("chan", "band"), split_axis=0, concat_axis=0, tiled=True)
    width = local.shape[3]
    block = lax.axis_index("chan")
    block_count = partner.shape[1]
    own_partner = jnp.sum(
        jnp.where(jnp.arange(block_count, dtype=jnp.int32)[None, :] == block, partner, 0), axis=1
    )
    blank = jnp.zeros_like(local)
    carry = (blank, blank)
    piece = lax.all_gather(local, "chan", axis=3, tiled=True)
    span = piece.shape[3]
    chosen = []
    for round_index in range(2):
        placed = own_partner[round_index] * width
        inside = (placed >= 0) & (placed < span)
        window_rows = lax.dynamic_slice_in_dim(piece, jnp.clip(placed, 0, span - width), width, 3)
        chosen.append(jnp.where(inside, window_rows, carry[round_index]))
    first_other = chosen[0]
    second_other = chosen[1]
    factor = 1.0 / (W * math.sqrt(local.shape[0]))

    def stack_pair(other_rows):
        product = jnp.einsum(
            "wpfi,wqfj->fpqij", local, other_rows, preferred_element_type=jnp.float32
        )
        real_part = product[:, 0, 0] + product[:, 1, 1]
        imag_part = product[:, 1, 0] - product[:, 0, 1]
        return jnp.stack([real_part, imag_part]) * factor

    return jnp.stack([stack_pair(first_other), stack_pair(second_other)])


def solution(mesh):
    return jax.shard_map(
        body,
        mesh=mesh,
        in_specs=(P(("chan", "band"), None, None), P(("chan", "band")), P(), P()),
        out_specs=P(None, None, "band", "chan", None),
        check_vma=False,
    )
```

profile of v0, /device:TPU:1, one launch (start us, length us, event | category | flops | bytes accessed | tf_op | source)
XLA Modules:
  0.0 218.0 jit_solution(3624640159972781501)
XLA Ops:
  6.5 0.0 all-gather.2.cloned.1.call-start
  6.6 1.2 sine_negate_fusion
  8.5 0.7 pad.4
  9.1 0.1 reshape.230
  9.2 0.8 convert_bitcast_fusion
  10.0 0.5 convert_element_type.34
  10.5 7.2 %fusion = f32[2560,256]{1,0:T(8,128)S(1)} fusion(bf16[2620,256]{1,0:T(8,128)(2,1)S(1)} %convert_element_type.34, bf16[1,2560,2747]{1,2,0:T(8,128)(2,1)} %param.4, s32[]{:T(128)S(6)} %select_n.35), kind=kOutput, calls=%fused_computation | convolution fusion | flops 3434086400 | bytes 17397764 | tf_op jit(solution)/shard_map/dot_general | solution.py:45
  17.7 0.0 copy-start.1
  17.7 0.0 copy-start.2
  17.7 1.5 fusion.4
  19.2 0.0 copy-done.1
  19.2 0.0 copy-done.2
  19.2 4.4 %convolution_convert_fusion = bf16[256,2560]{1,0:T(8,128)(2,1)S(1)} fusion(f32[2560,256]{1,0:T(8,128)S(1)} %fusion.4, f32[256,128]{1,0:T(8,128)S(1)} %copy-done.1, f32[256,128]{1,0:T(8,128)S(1)} %copy-done.2), kind=kOutput, calls=%fused_computation.8 | convolution fusion | flops 2013986816 | bytes 4194304 | tf_op jit(solution)/shard_map/dot_general | solution.py:50
  23.6 2.6 %convert_element_type.36 = bf16[1,2,8,16,16,160]{5,4,3,2,1,0:T(8,128)(2,1)S(1)} reshape(bf16[256,2560]{1,0:T(8,128)(2,1)S(1)} %convolution_convert_fusion) | data formatting | bytes 2621440 | tf_op jit(solution)/shard_map/convert_element_type | solution.py:53
  26.2 0.7 copy.16
  26.9 2.4 %copy.17 = bf16[128,2,16,160]{3,1,2,0:T(2,128)(2,1)S(1)} copy(bf16[128,2,16,160]{3,2,1,0:T(8,128)(2,1)S(1)} %bitcast.54) | data formatting | bytes 2621440 | tf_op jit(solution)/shard_map/reshape | solution.py:73
  29.4 39.6 %all_to_all.5 = bf16[128,2,16,160]{3,1,2,0:T(2,128)(2,1)S(1)} all-to-all(bf16[128,2,16,160]{3,1,2,0:T(2,128)(2,1)S(1)} %copy.17), channel_id=1, replica_groups=mesh['chan'=16,'band'=8] {'chan','band'}, dimensions={0} | all-to-all | bytes 2621440 | tf_op jit(solution)/shard_map/all_to_all | solution.py:79
  68.9 3.8 %copy.18 = bf16[128,2,16,160]{0,3,1,2:T(8,128)(2,1)} copy(bf16[128,2,16,160]{3,1,2,0:T(2,128)(2,1)S(1)} %all_to_all.5) | data formatting | bytes 2621440 | tf_op jit(solution)/shard_map/all_to_all | solution.py:79
  72.8 0.0 all-gather.2.cloned.1.call-update
  72.8 0.1 select_reduce_fusion
  72.9 0.7 fusion.39
  74.9 107.6 %all-gather.2.cloned.1.call-done = bf16[128,2,16,2560]{0,3,1,2:T(8,128)(2,1)} async-done(((bf16[128,2,16,160]{0,3,1,2:T(8,128)(2,1)}), bf16[128,2,16,2560]{0,3,1,2:T(8,128)(2,1)}) %all-gather.2.cloned.1.call-update) | async-done | bytes 20971536 | tf_op jit(solution)/shard_map/all_gather | solution.py:88
  182.5 3.0 %convolution_bitcast_fusion.1 = f32[16,2,2,160,160]{3,4,1,2,0:T(8,128)S(1)} fusion(bf16[128,2,16,160,1]{3,1,2,0,4:T(2,128)(2,1)S(1)} %bitcast.52, bf16[128,2,16,2560]{0,3,1,2:T(8,128)(2,1)} %all-gather.2.cloned.1.call-done, s32[]{:T(128)} %bitcast.6, pred[]{:T(512)} %bitcast), kind=kOutput, calls=%fused_computation.11 | convolution fusion | flops 420085760 | bytes 9176064 | tf_op jit(solution)/shard_map/wpfi,wqfj->fpqij/dot_general | solution.py:101
  185.5 0.4 fusion.7
  185.9 0.4 fusion.9
  186.3 3.0 %convolution_bitcast_fusion = f32[16,2,2,160,160]{3,4,0,2,1:T(8,128)S(1)} fusion(bf16[128,2,16,160,1]{3,1,2,0,4:T(2,128)(2,1)S(1)} %bitcast.53, bf16[128,2,16,2560]{0,3,1,2:T(8,128)(2,1)} %all-gather.2.cloned.1.call-done, s32[]{:T(128)} %bitcast.14, pred[]{:T(512)} %bitcast.13), kind=kOutput, calls=%fused_computation.10 | convolution fusion | flops 420085760 | bytes 9176064 | tf_op jit(solution)/shard_map/wpfi,wqfj->fpqij/dot_general | solution.py:101
  189.4 2.3 %fusion.6 = (f32[1,1,16,160,160]{3,4,2,1,0:T(8,128)S(1)}, f32[1,1,16,160,160]{3,4,2,1,0:T(8,128)}) fusion(f32[16,2,2,160,160]{3,4,0,2,1:T(8,128)S(1)} %convolution_bitcast_fusion), kind=kLoop, calls=%fused_computation.15 | loop fusion | flops 819200 | bytes 9830400 | tf_op jit(solution)/shard_map/stack | solution.py:106
  191.7 0.8 maximum_multiply_fusion
  192.5 0.9 copy-done
  193.4 0.8 maximum_multiply_fusion.1
  194.3 4.8 %pad_maximum_fusion = f32[2,2,16,160,160]{3,4,2,1,0:T(8,128)} fusion(f32[1,2,16,160,160]{3,4,2,1,0:T(8,128)S(1)} %maximum_multiply_fusion.1, f32[1,2,16,160,160]{3,4,2,1,0:T(8,128)S(1)} %maximum_multiply_fusion), kind=kLoop, calls=%fused_computation.3 | loop fusion | flops 1638400 | bytes 13107200 | tf_op jit(solution)/shard_map/stack | solution.py:108
  199.1 12.1 %copy.24 = f32[2,2,16,160,160]{4,3,2,1,0:T(8,128)} copy(f32[2,2,16,160,160]{3,4,2,1,0:T(8,128)} %pad_maximum_fusion) | data formatting | bytes 13107200 | tf_op jit(solution)/shard_map/stack | solution.py:108
  (6 shorter events, 0.0 us)
Async XLA Ops:
  6.5 176.0 %all-gather.2.cloned.1.call-start = ((), (), s32[]{:S(2)}) async-start(), calls=%async_computation.1 | async-start | bytes 22282240 | tf_op jit(solution)/shard_map/all_gather | solution.py:88
  17.7 1.5 copy-start.1
  17.7 1.5 copy-start.2
  68.9 3.9 %copy-start.3 = (s32[2,16]{1,0:T(2,128)S(1)}, s32[2,16]{1,0:T(2,128)}, u32[]{:S(2)}) copy-start(s32[2,16]{1,0:T(2,128)} %param.7) | copy-start | bytes 388
  191.7 1.7 copy-start
Sparse Core Ops, SparseCore 0:
  72.9 109.5 all-gather.1
where the time goes:
time: 218 us
  waiting for transfers between devices  108 us (50%)
  blocking collectives  39.6 us (18%)
  local copies, waits for them, and re-layouts  24.4 us (11%)
  matrix products  19.9 us (9%)
  between operations  15.5 us (7%)
  other arithmetic  11 us (5%)
    all_gather x1, waiting for transfers between devices, body(): piece = lax.all_gather(local, 'chan', axis=3, tiled=True)  108 us
    all_to_all x1, blocking collectives, body(): lax.all_to_all(arranged, ('chan', 'band'), split_axis=0, concat_axis=0, t...  39.6 us
    another operation x1, local copies, waits for them, and re-layouts, body(): return jnp.stack([stack_pair(first_other), stack_pair(second_other)])  12.1 us
    dot_general x1, matrix products, window_spectrum(): decimated = jnp.dot(piece, table, preferred_element_type=jnp.float32)  7.16 us
    dot_general x2, matrix products, stack_pair(): jnp.einsum('wpfi,wqfj->fpqij', local, other_rows, preferred_element_type=...  6.08 us
    another operation x1, other arithmetic, body(): return jnp.stack([stack_pair(first_other), stack_pair(second_other)])  4.8 us
    dot_general x1, matrix products, window_spectrum(): lax.dot_general(transform, normed, (((0,), (1,)), ((), ())), precision=la...  4.41 us
  transfers between devices with their start and end apart: 1, of which 1 were waited for; matrix products, arithmetic and copies ran while one was open for 0% of the time, Pallas kernels for 0%

commit v1 on v0

--- a/solution.py
+++ b/solution.py
@@ -85,7 +85,9 @@
     )
     blank = jnp.zeros_like(local)
     carry = (blank, blank)
-    piece = lax.all_gather(local, "chan", axis=3, tiled=True)
+    piece = jnp.concatenate(
+        lax.all_to_all(jnp.stack([local] * lax.axis_size("chan")), "chan", 0, 0), axis=3
+    )
     span = piece.shape[3]
     chosen = []
     for round_index in range(2):

time: 218 us -> 454 us (2.08)
  waiting for transfers between devices: 108 us -> 323 us
  local copies, waits for them, and re-layouts: 24.4 us -> 48.7 us
  between operations: 15.5 us -> 2.14 us
  starting transfers between devices: 0.01 us -> 7.35 us
    all_to_all x0 -> x1, waiting for transfers between devices: none -> 323 us  [body(): lax.all_to_all(jnp.stack([local] * lax.axis_size('chan')), 'chan', 0, 0)]
    all_gather x1 -> x0, waiting for transfers between devices: 108 us -> none  [body(): piece = lax.all_gather(local, 'chan', axis=3, tiled=True)]
    reshape x0 -> x1, local copies, waits for them, and re-layouts: none -> 11.7 us  [body(): jnp.concatenate(lax.all_to_all(jnp.stack([local] * lax.axis_size('chan'))...]
    another operation x0 -> x1, local copies, waits for them, and re-layouts: none -> 8.08 us  [body(): jnp.stack([local] * lax.axis_size('chan'))]
    all_to_all x0 -> x1, starting transfers between devices: none -> 7.35 us  [body(): lax.all_to_all(jnp.stack([local] * lax.axis_size('chan')), 'chan', 0, 0)]
    unnamed x8 -> x14, local copies, waits for them, and re-layouts: 0.91 us -> 7.09 us
where the time goes in v1:
time: 454 us; the launch traced here: 452 us
  waiting for transfers between devices  323 us (71%)
  local copies, waits for them, and re-layouts  48.7 us (11%)
  blocking collectives  39.6 us (9%)
  matrix products  18.6 us (4%)
  other arithmetic  12.9 us (3%)
  starting transfers between devices  7.35 us (2%)
    all_to_all x1, waiting for transfers between devices, body(): lax.all_to_all(jnp.stack([local] * lax.axis_size('chan')), 'chan', 0, 0)  323 us
    all_to_all x1, blocking collectives, body(): lax.all_to_all(arranged, ('chan', 'band'), split_axis=0, concat_axis=0, t...  39.6 us
    another operation x1, local copies, waits for them, and re-layouts, body(): return jnp.stack([stack_pair(first_other), stack_pair(second_other)])  12.1 us
    reshape x1, local copies, waits for them, and re-layouts, body(): jnp.concatenate(lax.all_to_all(jnp.stack([local] * lax.axis_size('chan'))...  11.7 us
  transfers between devices with their start and end apart: 1, of which 1 were waited for; matrix products, arithmetic and copies ran while one was open for 0% of the time, Pallas kernels for 0%

profile of v1, /device:TPU:1, one launch (start us, length us, event | category | flops | bytes accessed | tf_op | source)
XLA Modules:
  0.0 452.3 jit_solution(15034331084163549206)
XLA Ops:
  0.0 1.2 sine_negate_fusion
  1.9 0.7 pad.4
  2.6 0.1 reshape.240
  2.7 0.8 convert_bitcast_fusion
  3.5 0.5 convert_element_type.34
  4.0 7.2 %fusion = f32[2560,256]{1,0:T(8,128)S(1)} fusion(bf16[2620,256]{1,0:T(8,128)(2,1)S(1)} %convert_element_type.34, bf16[1,2560,2747]{1,2,0:T(8,128)(2,1)} %param.4, s32[]{:T(128)S(6)} %select_n.35), kind=kOutput, calls=%fused_computation | convolution fusion | flops 3434086400 | bytes 17397764 | tf_op jit(solution)/shard_map/dot_general | solution.py:45
  11.1 0.0 copy-start.4
  11.2 1.5 fusion.4
  12.7 4.4 convolution_convert_fusion
  17.1 2.6 convert_element_type.36
  19.7 0.7 copy.16
  20.4 2.4 copy.17
  22.8 39.6 %all_to_all.10 = bf16[128,2,16,160]{3,1,2,0:T(2,128)(2,1)S(1)} all-to-all(bf16[128,2,16,160]{3,1,2,0:T(2,128)(2,1)S(1)} %copy.17), channel_id=1, replica_groups=mesh['chan'=16,'band'=8] {'chan','band'}, dimensions={0} | all-to-all | bytes 2621440 | tf_op jit(solution)/shard_map/all_to_all | solution.py:79
  62.4 2.1 copy.18
  64.5 8.1 %stack.16 = bf16[16,128,2,16,160]{1,4,2,3,0:T(8,128)(2,1)} broadcast(bf16[128,2,16,160]{0,3,1,2:T(8,128)(2,1)S(1)} %copy.18), dimensions={1,2,3,4} | broadcast | bytes 22282240 | tf_op jit(solution)/shard_map/stack | solution.py:89
  72.6 7.3 %all-to-all-start.1 = ((bf16[16,128,2,16,160]{1,4,2,3,0:T(8,128)(2,1)}), bf16[16,128,2,16,160]{1,4,2,3,0:T(8,128)(2,1)}, u32[]{:S(2)}, u32[]{:S(2)}) async-start(bf16[16,128,2,16,160]{1,4,2,3,0:T(8,128)(2,1)} %stack.16), calls=%async_computation.1 | async-start | bytes 41943040 | tf_op jit(solution)/shard_map/all_to_all | solution.py:89
  80.0 0.1 select_reduce_fusion
  80.1 0.6 fusion.39
  82.0 323.0 %all-to-all-done.1 = bf16[16,128,2,16,160]{1,4,2,3,0:T(8,128)(2,1)} async-done(((bf16[16,128,2,16,160]{1,4,2,3,0:T(8,128)(2,1)}), bf16[16,128,2,16,160]{1,4,2,3,0:T(8,128)(2,1)}, u32[]{:S(2)}, u32[]{:S(2)}) %all-to-all-start.1) | async-done | bytes 20971552 | tf_op jit(solution)/shard_map/all_to_all | solution.py:89
  405.0 11.7 %copy.19 = bf16[128,2,16,16,160]{0,4,3,1,2:T(8,128)(2,1)S(1)} copy(bf16[128,2,16,16,160]{0,4,1,2,3:T(8,128)(2,1)} %bitcast.6) | data formatting | bytes 41943040 | tf_op jit(solution)/shard_map/reshape | solution.py:88
  416.7 1.8 convolution_bitcast_fusion.1
  418.5 5.2 %copy-done = bf16[128,2,16,16,160]{0,4,3,1,2:T(8,128)(2,1)} copy-done((bf16[128,2,16,16,160]{0,4,3,1,2:T(8,128)(2,1)}, bf16[128,2,16,16,160]{0,4,3,1,2:T(8,128)(2,1)S(1)}, u32[]{:S(2)}) %copy-start) | copy-done | bytes 20971544
  423.7 0.4 fusion.7
  424.1 1.9 fusion.9
  426.0 3.0 convolution_bitcast_fusion
  429.0 3.3 fusion.6
  432.3 0.6 maximum_multiply_fusion
  433.0 1.1 copy-done.2
  434.1 0.8 copy-done.3
  434.9 0.5 maximum_multiply_fusion.1
  435.4 4.8 %pad_maximum_fusion = f32[2,2,16,160,160]{3,4,2,1,0:T(8,128)} fusion(f32[1,2,16,160,160]{3,4,2,1,0:T(8,128)S(1)} %maximum_multiply_fusion.1, f32[1,2,16,160,160]{3,4,2,1,0:T(8,128)S(1)} %maximum_multiply_fusion), kind=kLoop, calls=%fused_computation.3 | loop fusion | flops 1638400 | bytes 13107200 | tf_op jit(solution)/shard_map/stack | solution.py:110
  440.2 12.1 %copy.25 = f32[2,2,16,160,160]{4,3,2,1,0:T(8,128)} copy(f32[2,2,16,160,160]{3,4,2,1,0:T(8,128)} %pad_maximum_fusion) | data formatting | bytes 13107200 | tf_op jit(solution)/shard_map/stack | solution.py:110
  (13 shorter events, 0.1 us)
Async XLA Ops:
  11.1 1.5 copy-start.4
  11.1 1.5 copy-start.5
  72.6 7.4 %copy-start.6 = (s32[2,16]{1,0:T(2,128)S(1)}, s32[2,16]{1,0:T(2,128)}, u32[]{:S(2)}) copy-start(s32[2,16]{1,0:T(2,128)} %param.7) | copy-start | bytes 388
  72.6 332.4 %all-to-all-start.1 = ((bf16[16,128,2,16,160]{1,4,2,3,0:T(8,128)(2,1)}), bf16[16,128,2,16,160]{1,4,2,3,0:T(8,128)(2,1)}, u32[]{:S(2)}, u32[]{:S(2)}) async-start(bf16[16,128,2,16,160]{1,4,2,3,0:T(8,128)(2,1)} %stack.16), calls=%async_computation.1 | async-start | bytes 41943040 | tf_op jit(solution)/shard_map/all_to_all | solution.py:89
  416.7 7.0 %copy-start = (bf16[128,2,16,16,160]{0,4,3,1,2:T(8,128)(2,1)}, bf16[128,2,16,16,160]{0,4,3,1,2:T(8,128)(2,1)S(1)}, u32[]{:S(2)}) copy-start(bf16[128,2,16,16,160]{0,4,3,1,2:T(8,128)(2,1)S(1)} %copy.19) | copy-start | bytes 62914564
  429.0 3.3 copy-start.1
  432.3 1.7 copy-start.2
  432.3 2.5 copy-start.3
